TPU v7x, 32 devices: a whole 2x2x4 slice. The times are simulated.
32 devices in a mesh: band: 2 (over y), domain: 16 (over z, x, core).
Axes of the slice: x: 2, y: 2, z: 4, core: 2. Of those that a mesh axis runs over, the one named last changes fastest.
Arguments:
- orbitals: bfloat16 [128, 16, 32, 256], P('domain', None, None, 'band'), may hold values from -12 to 12
- potential: float32 [128, 16, 32], P('domain'), may hold values from -2 to 0
Outputs:
- filtered: bfloat16 [128, 16, 32, 256], P('domain', None, None, 'band')
- correlation: float32 [256, 256], P('band')
- projected: float32 [256, 256], P('band')
All inputs are finite; a program needn't handle non-finite values.
Results may differ from a plain program's by a relative error of at most 0.005.
Values may be sent and summed in bfloat16 or wider, within the bound.
No kernel may reach another device: no remote copies, remote signals or barrier semaphores. Data moves between devices by JAX's collectives and lax.ppermute only.
A program may use at most 64 MiB of HBM per device.

v0:
```python
import jax
import jax.numpy as jnp
from jax import lax
from jax.sharding import PartitionSpec as P

RADIUS = 4
stencil_weights = (-205.0 / 72.0, 8.0 / 5.0, -1.0 / 5.0, 8.0 / 315.0, -1.0 / 560.0)
spectrum_centre = 6.0
first_factor = -0.125
second_factor = -1.0 / 7.0
memory_factor = -1.0 / 7.0


def padded(block, sides, width):
    for axis, dim in sides:
        count = lax.axis_size(axis)
        forward = [(i, i + 1) for i in range(count - 1)]
        forward.append((count - 1, 0))
        backward = [(target, source) for source, target in forward]
        low = lax.ppermute(
            lax.slice_in_dim(block, block.shape[dim] - width, None, axis=dim), axis, forward
        )
        high = lax.ppermute(lax.slice_in_dim(block, 0, width, axis=dim), axis, backward)
        block = jnp.concatenate([low, block, high], axis=dim)
    return block


def planes_of(extended, first_plane, planes):
    return lax.slice_in_dim(extended, first_plane, first_plane + planes, axis=0)


def hamiltonian(extended, potential, planes):
    middle = planes_of(extended, RADIUS, planes)
    summed = 3.0 * stencil_weights[0] * middle
    for offset in range(1, RADIUS + 1):
        beside = planes_of(extended, RADIUS + offset, planes) + planes_of(
            extended, RADIUS - offset, planes
        )
        beside = beside + jnp.roll(middle, offset, axis=1) + jnp.roll(middle, -offset, axis=1)
        beside = beside + jnp.roll(middle, offset, axis=2) + jnp.roll(middle, -offset, axis=2)
        summed = summed + stencil_weights[offset] * beside
    return -0.5 * summed + potential[:, :, :, None] * middle


def widened(values):
    return padded(values, (("domain", 0),), RADIUS)


def energy_block(filtered, potential, cell_count):
    extended = padded(filtered, (("domain", 0),), RADIUS).astype(jnp.float32)
    applied = hamiltonian(extended, potential, filtered.shape[0]).astype(jnp.bfloat16)
    return applied.reshape(cell_count, filtered.shape[3])


def shards(orbitals, potential):
    planes = orbitals.shape[0]
    initial = orbitals.astype(jnp.float32)
    extended = widened(orbitals).astype(jnp.float32)
    first = (
        (hamiltonian(extended, potential, planes) - spectrum_centre * initial) * first_factor
    ).astype(jnp.bfloat16)
    first_wide = widened(first).astype(jnp.float32)
    first_own = planes_of(first_wide, RADIUS, planes)
    filtered = (
        (hamiltonian(first_wide, potential, planes) - spectrum_centre * first_own) * second_factor
        + memory_factor * initial
    ).astype(jnp.bfloat16)
    cell_count = planes * filtered.shape[1] * filtered.shape[2]
    cell_weight = 1.0 / (cell_count * lax.axis_size("domain"))
    own_block = filtered.reshape(cell_count, filtered.shape[3])
    applied = energy_block(filtered, potential, cell_count)
    piece = lax.all_gather(own_block, "band", axis=1, tiled=True)
    correlation_piece = jnp.einsum(
        "cb,ck->bk", own_block, piece, preferred_element_type=jnp.float32
    )
    energy_piece = jnp.einsum("cb,ck->bk", applied, piece, preferred_element_type=jnp.float32)
    partial_terms = jnp.stack((correlation_piece, energy_piece))
    summed = lax.psum(partial_terms, "domain") * cell_weight
    correlation = summed[0]
    projected = summed[1]
    return (filtered, correlation, projected)


def solution(mesh):
    placed = (P("domain", None, None, "band"), P("domain", None, None))
    return jax.shard_map(
        shards,
        mesh=mesh,
        in_specs=placed,
        out_specs=(P("domain", None, None, "band"), P("band", None), P("band", None)),
        check_vma=False,
    )
```

profile of v0, /device:TPU:1, one launch (start us, length us, event | category | flops | bytes accessed | tf_op | source)
XLA Modules:
  0.0 240.1 jit_solution(3765272262205652214)
XLA Ops:
  7.2 1.3 fusion.132
  8.7 2.6 %collective-permute-start = (bf16[4,16,32,128]{3,2,1,0:T(8,128)(2,1)S(1)}, bf16[4,16,32,128]{3,2,1,0:T(8,128)(2,1)S(1)}, u32[]{:S(2)}, u32[]{:S(2)}) collective-permute-start(bf16[4,16,32,128]{3,2,1,0:T(8,128)(2,1)S(1)} %get-tuple-element.103), channel_id=1, source_target_pairs={{0,1},{1,2},{2,3},{3,4},{4,5},{5,6},{6,7},{7,8},{8,9},{9,10},{10,1... | collective-permute-start | bytes 1572872 | tf_op jit(solution)/shard_map/ppermute | solution.py:20
  11.3 6.8 %collective-permute-done.1 = bf16[4,16,32,128]{3,2,1,0:T(8,128)(2,1)S(1)} collective-permute-done((bf16[4,16,32,128]{3,2,1,0:T(8,128)(2,1)S(1)}, bf16[4,16,32,128]{3,2,1,0:T(8,128)(2,1)S(1)}, u32[]{:S(2)}, u32[]{:S(2)}) %collective-permute-start.1) | collective-permute-done | bytes 524320 | tf_op jit(solution)/shard_map/ppermute | solution.py:23
  18.1 4.9 %collective-permute-done = bf16[4,16,32,128]{3,2,1,0:T(8,128)(2,1)S(1)} collective-permute-done((bf16[4,16,32,128]{3,2,1,0:T(8,128)(2,1)S(1)}, bf16[4,16,32,128]{3,2,1,0:T(8,128)(2,1)S(1)}, u32[]{:S(2)}, u32[]{:S(2)}) %collective-permute-start) | collective-permute-done | bytes 524320 | tf_op jit(solution)/shard_map/ppermute | solution.py:20
  23.4 2.5 %fusion.128 = (f32[8,15,32,128]{3,2,1,0:T(8,128)}, f32[8,15,32,128]{3,2,1,0:T(8,128)}) fusion(f32[16,16,32,128]{3,2,1,0:T(8,128)S(1)} %maximum_convert_fusion), kind=kLoop, calls=%fused_computation.157 | loop fusion | bytes 7864320 | tf_op jit(solution)/shard_map/jit(_roll_static)/slice | solution.py:39
  25.8 0.7 fusion.129
  26.5 0.6 fusion.127
  27.2 2.4 fusion.125
  29.6 0.8 fusion.126
  30.4 0.6 fusion.123
  31.1 0.8 fusion.124
  31.9 2.2 fusion.121
  34.1 0.8 fusion.122
  34.9 0.6 fusion.119
  35.5 0.9 fusion.120
  36.5 2.1 fusion.117
  38.6 0.9 fusion.118
  39.5 0.5 fusion.115
  40.0 0.9 fusion.116
  40.9 0.7 maximum_convert_fusion.7
  41.6 10.1 %fusion.2 = bf16[8,16,32,128]{3,2,1,0:T(8,128)(2,1)S(1)} fusion(bf16[8,16,32,128]{3,2,1,0:T(8,128)(2,1)S(1)} %copy-done.2, f32[16,16,32,128]{3,2,1,0:T(8,128)S(1)} %maximum_convert_fusion, f32[8,15,32,128]{3,2,1,0:T(8,128)} %get-tuple-element.90, f32[8,1,32,128]{3,2,1,0:T(8,128)} %get-tuple-element.92, f32[8,1,32,128]{3,2,1,0:T(8,128)} %get-tuple-element.91, ...), kind=kLoop, calls=%fused_computation.4 | loop fusion | flops 27787264 | bytes 54542336 | tf_op jit(solution)/shard_map/convert_element_type | solution.py:61
  51.7 2.4 %collective-permute-start.3 = (bf16[4,16,32,128]{3,2,1,0:T(8,128)(2,1)S(1)}, bf16[4,16,32,128]{3,2,1,0:T(8,128)(2,1)S(1)}, u32[]{:S(2)}, u32[]{:S(2)}) collective-permute-start(bf16[4,16,32,128]{3,2,1,0:T(8,128)(2,1)S(1)} %get-tuple-element.102), channel_id=1, source_target_pairs={{1,0},{2,1},{3,2},{4,3},{5,4},{6,5},{7,6},{8,7},{9,8},{10,9},{11,1... | collective-permute-start | bytes 1572872 | tf_op jit(solution)/shard_map/ppermute | solution.py:23
  54.5 12.2 %collective-permute-done.3 = bf16[4,16,32,128]{3,2,1,0:T(8,128)(2,1)S(1)} collective-permute-done((bf16[4,16,32,128]{3,2,1,0:T(8,128)(2,1)S(1)}, bf16[4,16,32,128]{3,2,1,0:T(8,128)(2,1)S(1)}, u32[]{:S(2)}, u32[]{:S(2)}) %collective-permute-start.3) | collective-permute-done | bytes 524320 | tf_op jit(solution)/shard_map/ppermute | solution.py:23
  67.1 2.5 %fusion.113 = (f32[8,15,32,128]{3,2,1,0:T(8,128)}, f32[8,15,32,128]{3,2,1,0:T(8,128)}) fusion(f32[16,16,32,128]{3,2,1,0:T(8,128)S(1)} %maximum_convert_fusion.1), kind=kLoop, calls=%fused_computation.142 | loop fusion | bytes 7864320 | tf_op jit(solution)/shard_map/jit(_roll_static)/slice | solution.py:39
  69.5 0.7 fusion.114
  70.2 0.6 fusion.112
  70.8 2.4 fusion.110
  73.2 0.8 fusion.111
  74.0 0.6 fusion.108
  74.7 0.8 fusion.109
  75.5 2.3 fusion.106
  77.8 0.6 fusion.104
  78.5 0.9 fusion.105
  79.4 2.1 fusion.102
  81.5 1.8 fusion.100
  83.3 0.9 fusion.101
  84.3 0.7 maximum_convert_fusion.5
  85.0 10.1 %fusion.4 = bf16[8,16,32,128]{3,2,1,0:T(8,128)(2,1)S(1)} fusion(bf16[8,16,32,128]{3,2,1,0:T(8,128)(2,1)S(1)} %copy-done.2, f32[16,16,32,128]{3,2,1,0:T(8,128)S(1)} %maximum_convert_fusion.1, f32[8,15,32,128]{3,2,1,0:T(8,128)} %get-tuple-element.60, f32[8,1,32,128]{3,2,1,0:T(8,128)} %get-tuple-element.62, f32[8,1,32,128]{3,2,1,0:T(8,128)S(1)} %get-tuple-element.61, ...), kind=kLoop, calls=%fused_computation.6 | loop fusion | flops 28311552 | bytes 54542336 | tf_op jit(solution)/shard_map/convert_element_type | solution.py:67
  95.3 1.7 collective-permute-start.4
  97.3 12.6 %collective-permute-done.5 = bf16[4,16,32,128]{3,2,1,0:T(8,128)(2,1)S(1)} collective-permute-done((bf16[4,16,32,128]{3,2,1,0:T(8,128)(2,1)S(1)}, bf16[4,16,32,128]{3,2,1,0:T(8,128)(2,1)S(1)}, u32[]{:S(2)}, u32[]{:S(2)}) %collective-permute-start.5) | collective-permute-done | bytes 524320 | tf_op jit(solution)/shard_map/ppermute | solution.py:23
  109.9 1.6 maximum_convert_fusion.2
  111.5 2.5 %fusion.98 = (f32[8,15,32,128]{3,2,1,0:T(8,128)}, f32[8,15,32,128]{3,2,1,0:T(8,128)}) fusion(f32[16,16,32,128]{3,2,1,0:T(8,128)S(1)} %maximum_convert_fusion.2), kind=kLoop, calls=%fused_computation.127 | loop fusion | bytes 7864320 | tf_op jit(solution)/shard_map/jit(_roll_static)/slice | solution.py:39
  113.9 0.7 fusion.99
  114.6 0.6 fusion.97
  115.3 2.4 fusion.95
  117.6 0.9 fusion.96
  118.5 0.6 fusion.93
  119.1 0.8 fusion.94
  120.0 1.5 fusion.91
  121.5 0.8 fusion.92
  122.3 0.9 fusion.90
  123.2 2.1 fusion.87
  125.4 1.1 fusion.88
  126.5 0.9 fusion.86
  127.4 0.7 maximum_convert_fusion.3
  128.1 0.6 fusion.89
  128.8 0.5 fusion.85
  129.2 10.8 %fusion.13 = bf16[8,16,32,128]{3,2,1,0:T(8,128)(2,1)} fusion(f32[16,16,32,128]{3,2,1,0:T(8,128)S(1)} %maximum_convert_fusion.2, f32[8,15,32,128]{3,2,1,0:T(8,128)} %get-tuple-element.30, f32[8,1,32,128]{3,2,1,0:T(8,128)} %get-tuple-element.32, f32[8,1,32,128]{3,2,1,0:T(8,128)} %get-tuple-element.31, f32[8,15,32,128]{3,2,1,0:T(8,128)} %get-tuple-element.29, ...), kind=kLoop, calls=%fused_computation.16 | loop fusion | flops 25690112 | bytes 53493760 | tf_op jit(solution)/shard_map/convert_element_type | solution.py:51
  140.1 2.2 convolution_bitcast_fusion.1
  142.6 0.5 convolution_bitcast_fusion
  143.1 0.7 pad_maximum_fusion
  143.9 87.7 %all-reduce.2.cloned.1.call-done = f32[2,128,256]{2,1,0:T(8,128)} async-done(((f32[2,128,256]{2,1,0:T(8,128)}), f32[2,128,256]{2,1,0:T(8,128)}) %all-reduce.2.cloned.1.call-update) | async-done | bytes 262160 | tf_op jit(solution)/shard_map/psum | solution.py:78
  231.6 1.0 broadcast_multiply_fusion
  232.5 0.7 slice_bitcast_fusion
  (28 shorter events, 2.1 us)
Async XLA Ops:
  7.2 15.9 %copy-start.2 = (bf16[8,16,32,128]{3,2,1,0:T(8,128)(2,1)S(1)}, bf16[8,16,32,128]{3,2,1,0:T(8,128)(2,1)}, u32[]{:S(2)}) copy-start(bf16[8,16,32,128]{3,2,1,0:T(8,128)(2,1)} %param.2) | copy-start | bytes 3145732
  7.2 132.9 %all-gather.2.cloned.1.call-start = ((), (), s32[]{:S(2)}) async-start(), calls=%async_computation | async-start | bytes 3145728 | tf_op jit(solution)/shard_map/all_gather | solution.py:72
  8.6 9.5 %collective-permute-start.1 = (bf16[4,16,32,128]{3,2,1,0:T(8,128)(2,1)S(1)}, bf16[4,16,32,128]{3,2,1,0:T(8,128)(2,1)S(1)}, u32[]{:S(2)}, u32[]{:S(2)}) collective-permute-start(bf16[4,16,32,128]{3,2,1,0:T(8,128)(2,1)S(1)} %get-tuple-element.104), channel_id=1, source_target_pairs={{1,0},{2,1},{3,2},{4,3},{5,4},{6,5},{7,6},{8,7},{9,8},{10,9},{11,1... | collective-permute-start | bytes 1572872 | tf_op jit(solution)/shard_map/ppermute | solution.py:23
  8.7 14.4 %collective-permute-start = (bf16[4,16,32,128]{3,2,1,0:T(8,128)(2,1)S(1)}, bf16[4,16,32,128]{3,2,1,0:T(8,128)(2,1)S(1)}, u32[]{:S(2)}, u32[]{:S(2)}) collective-permute-start(bf16[4,16,32,128]{3,2,1,0:T(8,128)(2,1)S(1)} %get-tuple-element.103), channel_id=1, source_target_pairs={{0,1},{1,2},{2,3},{3,4},{4,5},{5,6},{6,7},{7,8},{8,9},{9,10},{10,1... | collective-permute-start | bytes 1572872 | tf_op jit(solution)/shard_map/ppermute | solution.py:20
  40.0 1.6 copy-start.5
  51.7 15.0 %collective-permute-start.3 = (bf16[4,16,32,128]{3,2,1,0:T(8,128)(2,1)S(1)}, bf16[4,16,32,128]{3,2,1,0:T(8,128)(2,1)S(1)}, u32[]{:S(2)}, u32[]{:S(2)}) collective-permute-start(bf16[4,16,32,128]{3,2,1,0:T(8,128)(2,1)S(1)} %get-tuple-element.102), channel_id=1, source_target_pairs={{1,0},{2,1},{3,2},{4,3},{5,4},{6,5},{7,6},{8,7},{9,8},{10,9},{11,1... | collective-permute-start | bytes 1572872 | tf_op jit(solution)/shard_map/ppermute | solution.py:23
  54.2 12.6 %collective-permute-start.2 = (bf16[4,16,32,128]{3,2,1,0:T(8,128)(2,1)S(1)}, bf16[4,16,32,128]{3,2,1,0:T(8,128)(2,1)S(1)}, u32[]{:S(2)}, u32[]{:S(2)}) collective-permute-start(bf16[4,16,32,128]{3,2,1,0:T(8,128)(2,1)S(1)} %get-tuple-element.101), channel_id=1, source_target_pairs={{0,1},{1,2},{2,3},{3,4},{4,5},{5,6},{6,7},{7,8},{8,9},{9,10},{10,1... | collective-permute-start | bytes 1572872 | tf_op jit(solution)/shard_map/ppermute | solution.py:20
  95.1 1.9 copy-start
  95.2 14.7 %collective-permute-start.5 = (bf16[4,16,32,128]{3,2,1,0:T(8,128)(2,1)S(1)}, bf16[4,16,32,128]{3,2,1,0:T(8,128)(2,1)S(1)}, u32[]{:S(2)}, u32[]{:S(2)}) collective-permute-start(bf16[4,16,32,128]{3,2,1,0:T(8,128)(2,1)S(1)} %get-tuple-element.100), channel_id=1, source_target_pairs={{1,0},{2,1},{3,2},{4,3},{5,4},{6,5},{7,6},{8,7},{9,8},{10,9},{11,1... | collective-permute-start | bytes 1572872 | tf_op jit(solution)/shard_map/ppermute | solution.py:23
  95.3 14.6 %collective-permute-start.4 = (bf16[4,16,32,128]{3,2,1,0:T(8,128)(2,1)S(1)}, bf16[4,16,32,128]{3,2,1,0:T(8,128)(2,1)S(1)}, u32[]{:S(2)}, u32[]{:S(2)}) collective-permute-start(bf16[4,16,32,128]{3,2,1,0:T(8,128)(2,1)S(1)} %get-tuple-element.99), channel_id=1, source_target_pairs={{0,1},{1,2},{2,3},{3,4},{4,5},{5,6},{6,7},{7,8},{8,9},{9,10},{10,1... | collective-permute-start | bytes 1572872 | tf_op jit(solution)/shard_map/ppermute | solution.py:20
  97.0 134.5 %all-reduce.2.cloned.1.call-start = ((), (), s32[]{:S(2)}) async-start(), calls=%async_computation.1 | async-start | bytes 524288 | tf_op jit(solution)/shard_map/psum | solution.py:78
  125.4 2.0 copy-start.1
  140.1 2.3 copy-start.4
  140.1 2.5 %copy-start.3 = (bf16[4096,256]{1,0:T(8,128)(2,1)S(1)}, bf16[4096,256]{1,0:T(8,128)(2,1)}, u32[]{:S(2)}) copy-start(bf16[4096,256]{1,0:T(8,128)(2,1)} %all-gather.2.cloned.1.call-done) | copy-start | bytes 6291460
Sparse Core Ops, SparseCore 0:
  97.2 33.2 all-gather.1
  144.0 87.4 all-reduce.1
where the time goes:
time: 240 us
  waiting for transfers between devices  124 us (52%)
  local copies, waits for them, and re-layouts  54.1 us (23%)
  other arithmetic  37 us (15%)
  between operations  14.3 us (6%)
  starting transfers between devices  7.59 us (3%)
  matrix products  2.76 us (1%)
    psum x1, waiting for transfers between devices, shards(): summed = lax.psum(partial_terms, 'domain') * cell_weight  87.7 us
    slice x24, local copies, waits for them, and re-layouts, hamiltonian(): jnp.roll(middle, -offset, axis=1)  35.2 us
    ppermute x3, waiting for transfers between devices, padded(): lax.ppermute(lax.slice_in_dim(block, 0, width, axis=dim), axis, backward)  31.6 us
    slice x21, local copies, waits for them, and re-layouts, hamiltonian(): jnp.roll(middle, -offset, axis=2)  16.5 us
    convert_element_type x1, other arithmetic, energy_block(): hamiltonian(extended, potential, filtered.shape[0]).astype(jnp.bfloat16)  10.8 us
    convert_element_type x1, other arithmetic, shards(): filtered = ((hamiltonian(first_wide, potential, planes) - spectrum_centre...  10.1 us
    convert_element_type x1, other arithmetic, shards(): first = ((hamiltonian(extended, potential, planes) - spectrum_centre * in...  10.1 us
    ppermute x3, waiting for transfers between devices, padded(): lax.ppermute(lax.slice_in_dim(block, block.shape[dim] - width, None, axis...  4.95 us
  transfers between devices with their start and end apart: 8, of which 5 were waited for; matrix products, arithmetic and copies ran while one was open for 13% of the time, Pallas kernels for 0%

commit v1 on v0

--- a/solution.py
+++ b/solution.py
@@ -75,7 +75,7 @@
     )
     energy_piece = jnp.einsum("cb,ck->bk", applied, piece, preferred_element_type=jnp.float32)
     partial_terms = jnp.stack((correlation_piece, energy_piece))
-    summed = lax.psum(partial_terms, "domain") * cell_weight
+    summed = jnp.sum(lax.all_gather(partial_terms, "domain"), axis=0) * cell_weight
     correlation = summed[0]
     projected = summed[1]
     return (filtered, correlation, projected)

time: 240 us -> 204 us (0.85)
  waiting for transfers between devices: 124 us -> 85.8 us
    psum x1 -> x0, waiting for transfers between devices: 87.7 us -> none  [shards(): summed = lax.psum(partial_terms, 'domain') * cell_weight]
    all_gather x0 -> x1, waiting for transfers between devices: none -> 49.1 us  [shards(): lax.all_gather(partial_terms, 'domain')]
    reduce_sum x0 -> x1, other arithmetic: none -> 2.48 us  [shards(): jnp.sum(lax.all_gather(partial_terms, 'domain'), axis=0) * cell_weight]
  transfers between devices with their start and end apart: 8 -> 8, of which waited for: 5 -> 5; matrix products, arithmetic and copies ran while one was open for 13% -> 15% of each run, Pallas kernels for 0% -> 0%
where the time goes in v1:
time: 204 us; the launch traced here: 203 us
  waiting for transfers between devices  85.8 us (42%)
  local copies, waits for them, and re-layouts  54.1 us (27%)
  other arithmetic  38.5 us (19%)
  between operations  14.3 us (7%)
  starting transfers between devices  7.59 us (4%)
  matrix products  2.76 us (1%)
    all_gather x1, waiting for transfers between devices, shards(): lax.all_gather(partial_terms, 'domain')  49.1 us
    slice x24, local copies, waits for them, and re-layouts, hamiltonian(): jnp.roll(middle, -offset, axis=1)  35.2 us
    ppermute x3, waiting for transfers between devices, padded(): lax.ppermute(lax.slice_in_dim(block, 0, width, axis=dim), axis, backward)  31.6 us
    slice x21, local copies, waits for them, and re-layouts, hamiltonian(): jnp.roll(middle, -offset, axis=2)  16.5 us
    convert_element_type x1, other arithmetic, energy_block(): hamiltonian(extended, potential, filtered.shape[0]).astype(jnp.bfloat16)  10.8 us
    convert_element_type x1, other arithmetic, shards(): filtered = ((hamiltonian(first_wide, potential, planes) - spectrum_centre...  10.1 us
    convert_element_type x1, other arithmetic, shards(): first = ((hamiltonian(extended, potential, planes) - spectrum_centre * in...  10.1 us
    ppermute x3, waiting for transfers between devices, padded(): lax.ppermute(lax.slice_in_dim(block, block.shape[dim] - width, None, axis...  4.95 us
  transfers between devices with their start and end apart: 8, of which 5 were waited for; matrix products, arithmetic and copies ran while one was open for 15% of the time, Pallas kernels for 0%

profile of v1, /device:TPU:1, one launch (start us, length us, event | category | flops | bytes accessed | tf_op | source)
XLA Modules:
  0.0 203.1 jit_solution(14241122247578907194)
XLA Ops:
  7.2 1.3 fusion.132
  8.7 2.6 %collective-permute-start = (bf16[4,16,32,128]{3,2,1,0:T(8,128)(2,1)S(1)}, bf16[4,16,32,128]{3,2,1,0:T(8,128)(2,1)S(1)}, u32[]{:S(2)}, u32[]{:S(2)}) collective-permute-start(bf16[4,16,32,128]{3,2,1,0:T(8,128)(2,1)S(1)} %get-tuple-element.103), channel_id=1, source_target_pairs={{0,1},{1,2},{2,3},{3,4},{4,5},{5,6},{6,7},{7,8},{8,9},{9,10},{10,1... | collective-permute-start | bytes 1572872 | tf_op jit(solution)/shard_map/ppermute | solution.py:20
  11.3 6.8 %collective-permute-done.1 = bf16[4,16,32,128]{3,2,1,0:T(8,128)(2,1)S(1)} collective-permute-done((bf16[4,16,32,128]{3,2,1,0:T(8,128)(2,1)S(1)}, bf16[4,16,32,128]{3,2,1,0:T(8,128)(2,1)S(1)}, u32[]{:S(2)}, u32[]{:S(2)}) %collective-permute-start.1) | collective-permute-done | bytes 524320 | tf_op jit(solution)/shard_map/ppermute | solution.py:23
  18.1 4.9 %collective-permute-done = bf16[4,16,32,128]{3,2,1,0:T(8,128)(2,1)S(1)} collective-permute-done((bf16[4,16,32,128]{3,2,1,0:T(8,128)(2,1)S(1)}, bf16[4,16,32,128]{3,2,1,0:T(8,128)(2,1)S(1)}, u32[]{:S(2)}, u32[]{:S(2)}) %collective-permute-start) | collective-permute-done | bytes 524320 | tf_op jit(solution)/shard_map/ppermute | solution.py:20
  23.4 2.5 %fusion.128 = (f32[8,15,32,128]{3,2,1,0:T(8,128)}, f32[8,15,32,128]{3,2,1,0:T(8,128)}) fusion(f32[16,16,32,128]{3,2,1,0:T(8,128)S(1)} %maximum_convert_fusion), kind=kLoop, calls=%fused_computation.157 | loop fusion | bytes 7864320 | tf_op jit(solution)/shard_map/jit(_roll_static)/slice | solution.py:39
  25.8 0.7 fusion.129
  26.5 0.6 fusion.127
  27.2 2.4 %fusion.125 = (f32[8,14,32,128]{3,2,1,0:T(8,128)}, f32[8,14,32,128]{3,2,1,0:T(8,128)}) fusion(f32[16,16,32,128]{3,2,1,0:T(8,128)S(1)} %maximum_convert_fusion), kind=kLoop, calls=%fused_computation.154 | loop fusion | bytes 7340032 | tf_op jit(solution)/shard_map/jit(_roll_static)/slice | solution.py:39
  29.6 0.8 fusion.126
  30.4 0.6 fusion.123
  31.1 0.8 fusion.124
  31.9 2.2 %fusion.121 = (f32[8,13,32,128]{3,2,1,0:T(8,128)}, f32[8,13,32,128]{3,2,1,0:T(8,128)}) fusion(f32[16,16,32,128]{3,2,1,0:T(8,128)S(1)} %maximum_convert_fusion), kind=kLoop, calls=%fused_computation.150 | loop fusion | bytes 6815744 | tf_op jit(solution)/shard_map/jit(_roll_static)/slice | solution.py:39
  34.1 0.8 fusion.122
  34.9 0.6 fusion.119
  35.5 0.9 fusion.120
  36.5 2.1 %fusion.117 = (f32[8,12,32,128]{3,2,1,0:T(8,128)}, f32[8,12,32,128]{3,2,1,0:T(8,128)}) fusion(f32[16,16,32,128]{3,2,1,0:T(8,128)S(1)} %maximum_convert_fusion), kind=kLoop, calls=%fused_computation.146 | loop fusion | bytes 6291456 | tf_op jit(solution)/shard_map/jit(_roll_static)/slice | solution.py:39
  38.6 0.9 fusion.118
  39.5 0.5 fusion.115
  40.0 0.9 fusion.116
  40.9 0.7 maximum_convert_fusion.7
  41.6 10.1 %fusion.2 = bf16[8,16,32,128]{3,2,1,0:T(8,128)(2,1)S(1)} fusion(bf16[8,16,32,128]{3,2,1,0:T(8,128)(2,1)S(1)} %copy-done.2, f32[16,16,32,128]{3,2,1,0:T(8,128)S(1)} %maximum_convert_fusion, f32[8,15,32,128]{3,2,1,0:T(8,128)} %get-tuple-element.90, f32[8,1,32,128]{3,2,1,0:T(8,128)} %get-tuple-element.92, f32[8,1,32,128]{3,2,1,0:T(8,128)} %get-tuple-element.91, ...), kind=kLoop, calls=%fused_computation.4 | loop fusion | flops 27787264 | bytes 54542336 | tf_op jit(solution)/shard_map/convert_element_type | solution.py:61
  51.7 2.4 %collective-permute-start.3 = (bf16[4,16,32,128]{3,2,1,0:T(8,128)(2,1)S(1)}, bf16[4,16,32,128]{3,2,1,0:T(8,128)(2,1)S(1)}, u32[]{:S(2)}, u32[]{:S(2)}) collective-permute-start(bf16[4,16,32,128]{3,2,1,0:T(8,128)(2,1)S(1)} %get-tuple-element.102), channel_id=1, source_target_pairs={{1,0},{2,1},{3,2},{4,3},{5,4},{6,5},{7,6},{8,7},{9,8},{10,9},{11,1... | collective-permute-start | bytes 1572872 | tf_op jit(solution)/shard_map/ppermute | solution.py:23
  54.5 12.2 %collective-permute-done.3 = bf16[4,16,32,128]{3,2,1,0:T(8,128)(2,1)S(1)} collective-permute-done((bf16[4,16,32,128]{3,2,1,0:T(8,128)(2,1)S(1)}, bf16[4,16,32,128]{3,2,1,0:T(8,128)(2,1)S(1)}, u32[]{:S(2)}, u32[]{:S(2)}) %collective-permute-start.3) | collective-permute-done | bytes 524320 | tf_op jit(solution)/shard_map/ppermute | solution.py:23
  67.1 2.5 %fusion.113 = (f32[8,15,32,128]{3,2,1,0:T(8,128)}, f32[8,15,32,128]{3,2,1,0:T(8,128)}) fusion(f32[16,16,32,128]{3,2,1,0:T(8,128)S(1)} %maximum_convert_fusion.1), kind=kLoop, calls=%fused_computation.142 | loop fusion | bytes 7864320 | tf_op jit(solution)/shard_map/jit(_roll_static)/slice | solution.py:39
  69.5 0.7 fusion.114
  70.2 0.6 fusion.112
  70.8 2.4 %fusion.110 = (f32[8,14,32,128]{3,2,1,0:T(8,128)}, f32[8,14,32,128]{3,2,1,0:T(8,128)}) fusion(f32[16,16,32,128]{3,2,1,0:T(8,128)S(1)} %maximum_convert_fusion.1), kind=kLoop, calls=%fused_computation.139 | loop fusion | bytes 7340032 | tf_op jit(solution)/shard_map/jit(_roll_static)/slice | solution.py:39
  73.2 0.8 fusion.111
  74.0 0.6 fusion.108
  74.7 0.8 fusion.109
  75.5 2.3 %fusion.106 = (f32[8,13,32,128]{3,2,1,0:T(8,128)}, f32[8,13,32,128]{3,2,1,0:T(8,128)}) fusion(f32[16,16,32,128]{3,2,1,0:T(8,128)S(1)} %maximum_convert_fusion.1), kind=kLoop, calls=%fused_computation.135 | loop fusion | bytes 6815744 | tf_op jit(solution)/shard_map/jit(_roll_static)/slice | solution.py:39
  77.8 0.6 fusion.104
  78.5 0.9 fusion.105
  79.4 2.1 %fusion.102 = (f32[8,12,32,128]{3,2,1,0:T(8,128)}, f32[8,12,32,128]{3,2,1,0:T(8,128)}) fusion(f32[16,16,32,128]{3,2,1,0:T(8,128)S(1)} %maximum_convert_fusion.1), kind=kLoop, calls=%fused_computation.131 | loop fusion | bytes 6291456 | tf_op jit(solution)/shard_map/jit(_roll_static)/slice | solution.py:39
  81.5 1.8 fusion.100
  83.3 0.9 fusion.101
  84.3 0.7 maximum_convert_fusion.5
  85.0 10.1 %fusion.4 = bf16[8,16,32,128]{3,2,1,0:T(8,128)(2,1)S(1)} fusion(bf16[8,16,32,128]{3,2,1,0:T(8,128)(2,1)S(1)} %copy-done.2, f32[16,16,32,128]{3,2,1,0:T(8,128)S(1)} %maximum_convert_fusion.1, f32[8,15,32,128]{3,2,1,0:T(8,128)} %get-tuple-element.60, f32[8,1,32,128]{3,2,1,0:T(8,128)} %get-tuple-element.62, f32[8,1,32,128]{3,2,1,0:T(8,128)S(1)} %get-tuple-element.61, ...), kind=kLoop, calls=%fused_computation.6 | loop fusion | flops 28311552 | bytes 54542336 | tf_op jit(solution)/shard_map/convert_element_type | solution.py:67
  95.3 1.7 collective-permute-start.4
  97.3 12.6 %collective-permute-done.5 = bf16[4,16,32,128]{3,2,1,0:T(8,128)(2,1)S(1)} collective-permute-done((bf16[4,16,32,128]{3,2,1,0:T(8,128)(2,1)S(1)}, bf16[4,16,32,128]{3,2,1,0:T(8,128)(2,1)S(1)}, u32[]{:S(2)}, u32[]{:S(2)}) %collective-permute-start.5) | collective-permute-done | bytes 524320 | tf_op jit(solution)/shard_map/ppermute | solution.py:23
  109.9 1.6 maximum_convert_fusion.2
  111.5 2.5 %fusion.98 = (f32[8,15,32,128]{3,2,1,0:T(8,128)}, f32[8,15,32,128]{3,2,1,0:T(8,128)}) fusion(f32[16,16,32,128]{3,2,1,0:T(8,128)S(1)} %maximum_convert_fusion.2), kind=kLoop, calls=%fused_computation.127 | loop fusion | bytes 7864320 | tf_op jit(solution)/shard_map/jit(_roll_static)/slice | solution.py:39
  113.9 0.7 fusion.99
  114.6 0.6 fusion.97
  115.3 2.4 %fusion.95 = (f32[8,14,32,128]{3,2,1,0:T(8,128)}, f32[8,14,32,128]{3,2,1,0:T(8,128)}) fusion(f32[16,16,32,128]{3,2,1,0:T(8,128)S(1)} %maximum_convert_fusion.2), kind=kLoop, calls=%fused_computation.124 | loop fusion | bytes 7340032 | tf_op jit(solution)/shard_map/jit(_roll_static)/slice | solution.py:39
  117.6 0.9 fusion.96
  118.5 0.6 fusion.93
  119.1 0.8 fusion.94
  120.0 1.5 fusion.91
  121.5 0.8 fusion.92
  122.3 0.9 fusion.90
  123.2 2.1 %fusion.87 = (f32[8,12,32,128]{3,2,1,0:T(8,128)}, f32[8,12,32,128]{3,2,1,0:T(8,128)}) fusion(f32[16,16,32,128]{3,2,1,0:T(8,128)S(1)} %maximum_convert_fusion.2), kind=kLoop, calls=%fused_computation.116 | loop fusion | bytes 6291456 | tf_op jit(solution)/shard_map/jit(_roll_static)/slice | solution.py:39
  125.4 1.1 fusion.88
  126.5 0.9 fusion.86
  127.4 0.7 maximum_convert_fusion.3
  128.1 0.6 fusion.89
  128.8 0.5 fusion.85
  129.2 10.8 %fusion.13 = bf16[8,16,32,128]{3,2,1,0:T(8,128)(2,1)} fusion(f32[16,16,32,128]{3,2,1,0:T(8,128)S(1)} %maximum_convert_fusion.2, f32[8,15,32,128]{3,2,1,0:T(8,128)} %get-tuple-element.30, f32[8,1,32,128]{3,2,1,0:T(8,128)} %get-tuple-element.32, f32[8,1,32,128]{3,2,1,0:T(8,128)} %get-tuple-element.31, f32[8,15,32,128]{3,2,1,0:T(8,128)} %get-tuple-element.29, ...), kind=kLoop, calls=%fused_computation.16 | loop fusion | flops 25690112 | bytes 53493760 | tf_op jit(solution)/shard_map/convert_element_type | solution.py:51
  140.1 2.2 %convolution_bitcast_fusion.1 = f32[1,128,256]{2,1,0:T(8,128)S(1)} fusion(bf16[4096,128]{1,0:T(8,128)(2,1)S(1)} %bitcast.16, bf16[4096,256]{1,0:T(8,128)(2,1)} %all-gather.4.cloned.1.call-done), kind=kOutput, calls=%fused_computation.103 | convolution fusion | flops 268435456 | bytes 3276800 | tf_op jit(solution)/shard_map/cb,ck->bk/dot_general | solution.py:73
  142.6 0.5 convolution_bitcast_fusion
  143.1 0.7 pad_maximum_fusion
  143.9 49.1 %all-gather.6.cloned.1.call-done = f32[32,128,256]{2,1,0:T(8,128)} async-done(((f32[2,128,256]{2,1,0:T(8,128)}), f32[32,128,256]{2,1,0:T(8,128)}) %all-gather.6.cloned.1.call-update) | async-done | bytes 4194320 | tf_op jit(solution)/shard_map/all_gather | solution.py:78
  193.0 2.5 %reduce_sum.9 = f32[2,128,256]{2,1,0:T(8,128)S(1)} reduce(f32[16,2,128,256]{3,2,1,0:T(8,128)} %bitcast.17, f32[]{:T(128)} %constant.9.clone.1), dimensions={0}, to_apply=%region_0.1 | reduce | flops 983040 | bytes 4456452 | tf_op jit(solution)/shard_map/reduce_sum | solution.py:78
  195.5 0.7 slice_bitcast_fusion
  (29 shorter events, 2.1 us)
Async XLA Ops:
  7.2 15.9 %copy-start.2 = (bf16[8,16,32,128]{3,2,1,0:T(8,128)(2,1)S(1)}, bf16[8,16,32,128]{3,2,1,0:T(8,128)(2,1)}, u32[]{:S(2)}) copy-start(bf16[8,16,32,128]{3,2,1,0:T(8,128)(2,1)} %param.2) | copy-start | bytes 3145732
  7.2 132.9 %all-gather.4.cloned.1.call-start = ((), (), s32[]{:S(2)}) async-start(), calls=%async_computation | async-start | bytes 3145728 | tf_op jit(solution)/shard_map/all_gather | solution.py:72
  8.6 9.5 %collective-permute-start.1 = (bf16[4,16,32,128]{3,2,1,0:T(8,128)(2,1)S(1)}, bf16[4,16,32,128]{3,2,1,0:T(8,128)(2,1)S(1)}, u32[]{:S(2)}, u32[]{:S(2)}) collective-permute-start(bf16[4,16,32,128]{3,2,1,0:T(8,128)(2,1)S(1)} %get-tuple-element.104), channel_id=1, source_target_pairs={{1,0},{2,1},{3,2},{4,3},{5,4},{6,5},{7,6},{8,7},{9,8},{10,9},{11,1... | collective-permute-start | bytes 1572872 | tf_op jit(solution)/shard_map/ppermute | solution.py:23
  8.7 14.4 %collective-permute-start = (bf16[4,16,32,128]{3,2,1,0:T(8,128)(2,1)S(1)}, bf16[4,16,32,128]{3,2,1,0:T(8,128)(2,1)S(1)}, u32[]{:S(2)}, u32[]{:S(2)}) collective-permute-start(bf16[4,16,32,128]{3,2,1,0:T(8,128)(2,1)S(1)} %get-tuple-element.103), channel_id=1, source_target_pairs={{0,1},{1,2},{2,3},{3,4},{4,5},{5,6},{6,7},{7,8},{8,9},{9,10},{10,1... | collective-permute-start | bytes 1572872 | tf_op jit(solution)/shard_map/ppermute | solution.py:20
  40.0 1.6 copy-start.5
  51.7 15.0 %collective-permute-start.3 = (bf16[4,16,32,128]{3,2,1,0:T(8,128)(2,1)S(1)}, bf16[4,16,32,128]{3,2,1,0:T(8,128)(2,1)S(1)}, u32[]{:S(2)}, u32[]{:S(2)}) collective-permute-start(bf16[4,16,32,128]{3,2,1,0:T(8,128)(2,1)S(1)} %get-tuple-element.102), channel_id=1, source_target_pairs={{1,0},{2,1},{3,2},{4,3},{5,4},{6,5},{7,6},{8,7},{9,8},{10,9},{11,1... | collective-permute-start | bytes 1572872 | tf_op jit(solution)/shard_map/ppermute | solution.py:23
  54.2 12.6 %collective-permute-start.2 = (bf16[4,16,32,128]{3,2,1,0:T(8,128)(2,1)S(1)}, bf16[4,16,32,128]{3,2,1,0:T(8,128)(2,1)S(1)}, u32[]{:S(2)}, u32[]{:S(2)}) collective-permute-start(bf16[4,16,32,128]{3,2,1,0:T(8,128)(2,1)S(1)} %get-tuple-element.101), channel_id=1, source_target_pairs={{0,1},{1,2},{2,3},{3,4},{4,5},{5,6},{6,7},{7,8},{8,9},{9,10},{10,1... | collective-permute-start | bytes 1572872 | tf_op jit(solution)/shard_map/ppermute | solution.py:20
  95.1 1.9 copy-start
  95.2 14.7 %collective-permute-start.5 = (bf16[4,16,32,128]{3,2,1,0:T(8,128)(2,1)S(1)}, bf16[4,16,32,128]{3,2,1,0:T(8,128)(2,1)S(1)}, u32[]{:S(2)}, u32[]{:S(2)}) collective-permute-start(bf16[4,16,32,128]{3,2,1,0:T(8,128)(2,1)S(1)} %get-tuple-element.100), channel_id=1, source_target_pairs={{1,0},{2,1},{3,2},{4,3},{5,4},{6,5},{7,6},{8,7},{9,8},{10,9},{11,1... | collective-permute-start | bytes 1572872 | tf_op jit(solution)/shard_map/ppermute | solution.py:23
  95.3 14.6 %collective-permute-start.4 = (bf16[4,16,32,128]{3,2,1,0:T(8,128)(2,1)S(1)}, bf16[4,16,32,128]{3,2,1,0:T(8,128)(2,1)S(1)}, u32[]{:S(2)}, u32[]{:S(2)}) collective-permute-start(bf16[4,16,32,128]{3,2,1,0:T(8,128)(2,1)S(1)} %get-tuple-element.99), channel_id=1, source_target_pairs={{0,1},{1,2},{2,3},{3,4},{4,5},{5,6},{6,7},{7,8},{8,9},{9,10},{10,1... | collective-permute-start | bytes 1572872 | tf_op jit(solution)/shard_map/ppermute | solution.py:20
  97.0 96.0 %all-gather.6.cloned.1.call-start = ((), (), s32[]{:S(2)}) async-start(), calls=%async_computation.1 | async-start | bytes 4456448 | tf_op jit(solution)/shard_map/all_gather | solution.py:78
  125.4 2.0 copy-start.1
  140.1 2.3 %copy-start.4 = (bf16[8,16,32,128]{3,2,1,0:T(8,128)(2,1)S(1)}, bf16[8,16,32,128]{3,2,1,0:T(8,128)(2,1)}, u32[]{:S(2)}) copy-start(bf16[8,16,32,128]{3,2,1,0:T(8,128)(2,1)} %fusion.13) | copy-start | bytes 3145732
  140.1 2.5 %copy-start.3 = (bf16[4096,256]{1,0:T(8,128)(2,1)S(1)}, bf16[4096,256]{1,0:T(8,128)(2,1)}, u32[]{:S(2)}) copy-start(bf16[4096,256]{1,0:T(8,128)(2,1)} %all-gather.4.cloned.1.call-done) | copy-start | bytes 6291460
Sparse Core Ops, SparseCore 0:
  97.2 33.2 all-gather.3
  144.0 48.9 all-gather.5
